TPU v7x, 256 devices: a whole 4x4x8 slice. The times are simulated.
256 devices in a mesh: dp: 16 (over y_hi, z), seq: 16 (over x, y_lo, core).
Axes of the slice: x: 4, y: 4 (y_hi: 2, y_lo: 2; y = y_hi * 2 + y_lo), z: 8, core: 2. Of those that a mesh axis runs over, the one named last changes fastest.
Arguments:
- queries: bfloat16 [16, 2048, 2048], P('dp', 'seq'), may hold values from -6 to 6
- key_states: bfloat16 [16, 2048, 2048], P('dp', 'seq'), may hold values from -6 to 6
- value_states: bfloat16 [16, 2048, 2048], P('dp', 'seq'), may hold values from -6 to 6
- cotangent: bfloat16 [16, 2048, 2048], P('dp', 'seq'), may hold values from -6 to 6
- filter_taps: float32 [7, 2048], replicated, may hold values from -3 to 3
Outputs:
- conv_output: bfloat16 [16, 2048, 2048], P('dp', 'seq')
- grad_queries: bfloat16 [16, 2048, 2048], P('dp', 'seq')
- grad_keys: bfloat16 [16, 2048, 2048], P('dp', 'seq')
- grad_values: bfloat16 [16, 2048, 2048], P('dp', 'seq')
- filter_gradient: float32 [7, 2048], replicated
All inputs are finite; a program needn't handle non-finite values.
Results may differ from a plain program's by a relative error of at most 0.015.
Values may be sent and summed in bfloat16 or wider, within the bound.
No kernel may reach another device: no remote copies, remote signals or barrier semaphores. Data moves between devices by JAX's collectives and lax.ppermute only.
A program may use at most 128 MiB of HBM per device.

v0:
```python
import jax
import jax.numpy as jnp
from jax import lax
from jax.sharding import PartitionSpec as P

HD = 128
TAPS = 7


def padded(value, width):
    peers = lax.axis_size("seq")
    length = value.shape[0]
    up = [(i, (i + 1) % peers) for i in range(peers)]
    down = [(j, i) for i, j in up]
    before = lax.ppermute(value[length - width :], "seq", up)
    after = lax.ppermute(value[:width], "seq", down)
    return jnp.concatenate([before, value, after], axis=0)


def butterfly_sum(value):
    axes = ("dp", "seq")
    peers = lax.axis_size("dp") * lax.axis_size("seq")
    bit = 1
    while bit < peers:
        pairs = [(i, i ^ bit) for i in range(peers)]
        value = value + lax.ppermute(value, axes, pairs)
        bit *= 2
    return value


def butterfly_gather(value):
    peers = lax.axis_size("seq")
    index = lax.axis_index("seq")
    bit = 1
    while bit < peers:
        pairs = [(i, i ^ bit) for i in range(peers)]
        other = lax.ppermute(value, "seq", pairs)
        upper = index & bit != 0
        value = jnp.where(
            upper, jnp.concatenate([other, value], axis=0), jnp.concatenate([value, other], axis=0)
        )
        bit *= 2
    return value


def on_device(queries, key_states, value_states, cotangent, filter_taps):
    tok_rows = queries.shape[1]
    channels = queries.shape[2]
    peers = lax.axis_size("seq")
    seq_total = tok_rows * peers
    head_count = channels // HD
    score_scale = HD ** (-0.5)
    half_width = (TAPS - 1) // 2
    local_q = queries[0]
    local_k = key_states[0]
    local_v = value_states[0]
    local_g = cotangent[0]
    grad_pad = padded(local_g, half_width)
    grad_sum = jnp.zeros((tok_rows, channels), jnp.float32)
    for tap_index in range(TAPS):
        start_row = 2 * half_width - tap_index
        grad_sum = grad_sum + filter_taps[tap_index] * grad_pad[
            start_row : start_row + tok_rows
        ].astype(jnp.float32)
    grad_attn = grad_sum.astype(jnp.bfloat16)

    def head_major(matrix):
        return matrix.reshape(tok_rows, head_count, HD).transpose(1, 0, 2)

    k_heads = lax.all_gather(head_major(local_k), "seq", axis=1, tiled=True)
    k_heads, local_v = lax.optimization_barrier((k_heads, local_v))
    v_heads = lax.all_gather(head_major(local_v), "seq", axis=1, tiled=True)
    q_heads = local_q.reshape(tok_rows, head_count, HD)
    d_heads = grad_attn.reshape(tok_rows, head_count, HD)
    device_index = lax.axis_index("seq")
    own_pos = device_index * tok_rows + jnp.arange(tok_rows, dtype=jnp.int32)
    all_pos = jnp.arange(seq_total, dtype=jnp.int32)
    visible = own_pos[:, None] >= all_pos[None, :]
    scores = (
        jnp.einsum("thd,hud->htu", q_heads, k_heads, preferred_element_type=jnp.float32)
        * score_scale
    )
    row_top = jnp.max(jnp.where(visible, scores, -jnp.inf), -1, keepdims=True)
    row_top, local_q2 = lax.optimization_barrier((row_top, local_q))
    qa_heads = lax.all_gather(head_major(local_q2), "seq", axis=1, tiled=True)
    raw = jnp.where(visible, jnp.exp(scores - row_top), 0.0)
    row_total = jnp.sum(raw, -1, keepdims=True)
    probs = raw / row_total
    probs_low = probs.astype(jnp.bfloat16)
    probs_low, grad_attn2 = lax.optimization_barrier((probs_low, grad_attn))
    da_heads = lax.all_gather(head_major(grad_attn2), "seq", axis=1, tiled=True)
    attended = jnp.einsum("htu,hud->thd", probs_low, v_heads, preferred_element_type=jnp.float32)
    attn_out = attended.astype(jnp.bfloat16).reshape(tok_rows, channels)
    dprob = jnp.einsum("thd,hud->htu", d_heads, v_heads, preferred_element_type=jnp.float32)
    row_delta = jnp.sum(probs * dprob, -1, keepdims=True)
    dscore = (probs * (dprob - row_delta) * score_scale).astype(jnp.bfloat16)
    grad_q = jnp.einsum("htu,hud->thd", dscore, k_heads, preferred_element_type=jnp.float32)
    grad_queries = grad_q.astype(jnp.bfloat16).reshape(tok_rows, channels)
    stats = jnp.stack([row_top[..., 0], row_total[..., 0], row_delta[..., 0]], 0)
    stats = butterfly_gather(stats.transpose(2, 0, 1)).transpose(1, 0, 2)
    top_all = stats[0].T[:, None, :]
    total_all = stats[1].T[:, None, :]
    delta_all = stats[2].T[:, None, :]
    kq_heads = head_major(local_k)
    kv_heads = head_major(local_v)
    key_visible = all_pos[None, :] >= own_pos[:, None]
    scores_t = (
        jnp.einsum("hud,htd->hut", kq_heads, qa_heads, preferred_element_type=jnp.float32)
        * score_scale
    )
    raw_t = jnp.where(key_visible, jnp.exp(scores_t - top_all), 0.0)
    probs_t = raw_t / total_all
    probs_low_t = probs_t.astype(jnp.bfloat16)
    dprob_t = jnp.einsum("hud,htd->hut", kv_heads, da_heads, preferred_element_type=jnp.float32)
    dscore_t = (probs_t * (dprob_t - delta_all) * score_scale).astype(jnp.bfloat16)
    grad_k = jnp.einsum("hut,htd->uhd", dscore_t, qa_heads, preferred_element_type=jnp.float32)
    grad_v = jnp.einsum("hut,htd->uhd", probs_low_t, da_heads, preferred_element_type=jnp.float32)
    grad_keys = grad_k.astype(jnp.bfloat16).reshape(tok_rows, channels)
    grad_values = grad_v.astype(jnp.bfloat16).reshape(tok_rows, channels)
    out_pad = padded(attn_out, half_width)
    conv_sum = jnp.zeros((tok_rows, channels), jnp.float32)
    filter_rows = []
    local_gf = local_g.astype(jnp.float32)
    for tap_index in range(TAPS):
        moved = out_pad[tap_index : tap_index + tok_rows].astype(jnp.float32)
        conv_sum = conv_sum + filter_taps[tap_index] * moved
        filter_rows.append(jnp.sum(moved * local_gf, 0))
    filter_gradient = butterfly_sum(jnp.stack(filter_rows, 0))
    conv_output = conv_sum.astype(jnp.bfloat16)
    return (
        conv_output[None],
        grad_queries[None],
        grad_keys[None],
        grad_values[None],
        filter_gradient,
    )


def solution(mesh):
    block = P("dp", "seq", None)
    in_specs = (block, block, block, block, P())
    out_specs = (block, block, block, block, P())
    return jax.shard_map(
        on_device, mesh=mesh, in_specs=in_specs, out_specs=out_specs, check_vma=False
    )
```

profile of v0, /device:TPU:1, one launch (start us, length us, event | category | flops | bytes accessed | tf_op | source)
XLA Modules:
  0.0 298.4 jit_solution(1885777955495145412)
XLA Ops:
  7.2 0.0 all-gather.5.cloned.1.call-start
  7.2 1.1 copy.119
  8.4 0.9 copy.127
  9.3 0.0 all-gather.7.cloned.1.call-start
  9.4 1.3 copy.80
  10.7 58.6 %all-gather.5.cloned.1.call-done = bf16[16,2048,128]{2,1,0:T(8,128)(2,1)} async-done(((bf16[16,128,128]{2,1,0:T(8,128)(2,1)}), bf16[16,2048,128]{2,1,0:T(8,128)(2,1)}) %all-gather.5.cloned.1.call-update) | async-done | bytes 8388624 | tf_op jit(solution)/shard_map/all_gather | solution.py:70
  69.3 1.0 copy.81
  70.3 0.0 all-gather.9.cloned.1.call-start
  70.4 1.3 copy.83
  71.7 1.1 copy.120
  72.9 1.0 iota_compare_fusion
  73.9 11.8 %fusion.1 = (f32[16,128]{1,0:T(8,128)S(1)}, f32[16,2048,128]{2,1,0:T(8,128)}) fusion(pred[128,2048]{0,1:T(8,128)(4,1)S(1)} %get-tuple-element.63, bf16[16,2048,128]{2,1,0:T(8,128)(2,1)} %all-gather.5.cloned.1.call-done, bf16[128,16,128]{2,1,0:T(8,128)(2,1)S(1)} %bitcast.140), kind=kOutput, calls=%fused_computation.4 | convolution fusion | flops 1086322688 | bytes 25960448 | tf_op jit(solution)/shard_map/thd,hud->htu/dot_general | solution.py:80
  85.7 1.0 copy.96
  86.7 0.0 all-gather.11.cloned.1.call-start
  86.8 0.3 copy.84
  87.0 0.2 slice_bitcast_fusion.1
  87.3 1.4 collective-permute-start.1
  88.7 0.4 collective-permute-start
  89.2 22.3 %collective-permute-done.1 = bf16[3,2048]{0,1:T(8,128)(2,1)S(1)} collective-permute-done((bf16[3,2048]{0,1:T(8,128)(2,1)S(1)}, bf16[3,2048]{0,1:T(8,128)(2,1)S(1)}, u32[]{:S(2)}, u32[]{:S(2)}) %collective-permute-start.1) | collective-permute-done | bytes 12320 | tf_op jit(solution)/shard_map/ppermute | solution.py:15
  111.5 3.4 %collective-permute-done = bf16[3,2048]{0,1:T(8,128)(2,1)S(1)} collective-permute-done((bf16[3,2048]{0,1:T(8,128)(2,1)S(1)}, bf16[3,2048]{0,1:T(8,128)(2,1)S(1)}, u32[]{:S(2)}, u32[]{:S(2)}) %collective-permute-start) | collective-permute-done | bytes 12320 | tf_op jit(solution)/shard_map/ppermute | solution.py:16
  114.9 3.7 %fusion.33 = bf16[128,2048]{0,1:T(8,128)(2,1)S(1)} fusion(bf16[128,2048]{0,1:T(8,128)(2,1)S(1)} %bitcast.122, bf16[3,2048]{0,1:T(8,128)(2,1)S(1)} %collective-permute-done.1, bf16[3,2048]{0,1:T(8,128)(2,1)S(1)} %collective-permute-done, f32[2048]{0:T(1024)S(1)} %bitcast.152, f32[2048]{0:T(1024)S(1)} %bitcast.154, f32[2048]{0:T(1024)S(1)} %bitcast.144, ...), kind=kLoop, calls=%fused_computation.66 | loop fusion | flops 10223616 | bytes 1130496 | tf_op jit(solution)/shard_map/convert_element_type | solution.py:65
  118.7 9.5 %fusion.5 = f32[16,128]{1,0:T(8,128)S(1)} fusion(f32[16,2048,128]{2,1,0:T(8,128)} %get-tuple-element.65, f32[16,128]{1,0:T(8,128)S(1)} %get-tuple-element.64, pred[128,2048]{0,1:T(8,128)(4,1)S(1)} %get-tuple-element.63), kind=kLoop, calls=%fused_computation.11 | loop fusion | flops 16775168 | bytes 17055744 | tf_op jit(solution)/shard_map/reduce_sum | solution.py:87
  128.2 10.3 %all-gather.7.cloned.1.call-done = bf16[16,2048,128]{2,1,0:T(8,128)(2,1)} async-done(((bf16[16,128,128]{2,1,0:T(8,128)(2,1)}), bf16[16,2048,128]{2,1,0:T(8,128)(2,1)}) %all-gather.7.cloned.1.call-update) | async-done | bytes 8388624 | tf_op jit(solution)/shard_map/all_gather | solution.py:72
  138.5 16.0 %multiply_reduce_fusion = (f32[16,128]{1,0:T(8,128)S(1)}, bf16[16,128,2048]{1,2,0:T(8,128)(2,1)}, f32[16,128,2048]{1,2,0:T(8,128)}) fusion(f32[16,128]{1,0:T(8,128)S(1)} %fusion.5, f32[16,128]{1,0:T(8,128)S(1)} %get-tuple-element.64, f32[16,2048,128]{2,1,0:T(8,128)} %get-tuple-element.65, pred[128,2048]{0,1:T(8,128)(4,1)S(1)} %get-tuple-element.63, ...), kind=kOutput, calls=%fused_computation.9 | convolution fusion | flops 1103099904 | bytes 51142656 | tf_op jit(solution)/shard_map/thd,hud->htu/dot_general | solution.py:94
  154.5 1.0 copy.97
  155.5 0.2 copy.104
  155.7 8.8 %multiply_reduce_fusion.1 = (f32[16,128]{1,0:T(8,128)S(1)}, bf16[128,16,128]{2,0,1:T(8,128)(2,1)S(1)}) fusion(f32[128,16,128]{2,0,1:T(8,128)S(1)} %copy.104, bf16[16,2048,128]{2,1,0:T(8,128)(2,1)} %all-gather.7.cloned.1.call-done, bf16[16,128,2048]{1,2,0:T(8,128)(2,1)} %get-tuple-element.14), kind=kOutput, calls=%fused_computation.73 | convolution fusion | flops 1074788352 | bytes 18358272 | tf_op jit(solution)/shard_map/htu,hud->thd/dot_general | solution.py:92
  164.5 0.1 collective-permute-start.2
  164.6 1.1 copy.90
  165.7 0.6 collective-permute-start.3
  166.3 0.3 copy.88
  166.6 0.3 copy.89
  166.9 19.5 %collective-permute-done.3 = bf16[3,2048]{0,1:T(8,128)(2,1)S(1)} collective-permute-done((bf16[3,2048]{0,1:T(8,128)(2,1)}, bf16[3,2048]{0,1:T(8,128)(2,1)S(1)}, u32[]{:S(2)}, u32[]{:S(2)}) %collective-permute-start.3) | collective-permute-done | bytes 12320 | tf_op jit(solution)/shard_map/ppermute | solution.py:16
  186.4 3.4 %fusion.39 = (f32[2048]{0:T(1024)S(1)}, f32[2048]{0:T(1024)S(1)}, f32[2048]{0:T(1024)S(1)}, f32[2048]{0:T(1024)S(1)}, f32[2048]{0:T(1024)S(1)}, /*index=5*/f32[2048]{0:T(1024)S(1)}) fusion(bf16[3,2048]{0,1:T(8,128)(2,1)S(1)} %collective-permute-done.3, bf16[128,2048]{0,1:T(8,128)(2,1)S(1)} %bitcast.125, bf16[1,128,2048]{1,2,0:T(8,128)(2,1)S(1)} %copy.84, ...), kind=kLoop, calls=%fused_computation.72 | loop fusion | flops 9687040 | bytes 1122304 | tf_op jit(solution)/shard_map/reduce_sum | solution.py:127
  189.8 0.1 stack.35
  189.9 0.1 collective-permute-start.8
  190.1 0.5 collective-permute-start.4
  190.5 0.7 collective-permute-done.8
  191.3 0.3 collective-permute-start.9
  191.6 1.3 collective-permute-start.5
  193.0 3.8 %collective-permute-done.9 = f32[7,2048]{1,0:T(8,128)S(1)} collective-permute-done((f32[7,2048]{1,0:T(8,128)S(1)}, f32[7,2048]{1,0:T(8,128)S(1)}, u32[]{:S(2)}, u32[]{:S(2)}) %collective-permute-start.9) | collective-permute-done | bytes 57376 | tf_op jit(solution)/shard_map/ppermute | solution.py:26
  196.8 0.1 collective-permute-start.10
  196.9 2.0 collective-permute-done.5
  198.9 0.1 collective-permute-start.6
  199.0 1.4 collective-permute-done.10
  200.4 2.4 collective-permute-start.11
  202.8 17.1 %fusion.20 = bf16[16,128,128]{2,1,0:T(8,128)(2,1)S(1)} fusion(bf16[16,2048,128]{2,1,0:T(8,128)(2,1)} %all-gather.5.cloned.1.call-done, f32[16,128,2048]{1,2,0:T(8,128)} %get-tuple-element.66, f32[16,128]{1,0:T(8,128)S(1)} %get-tuple-element.46, f32[16,2048,128]{2,1,0:T(8,128)} %get-tuple-element.65, f32[16,128]{1,0:T(8,128)S(1)} %fusion.5, ...), kind=kOutput, calls=%fused_computation.37 | convolution fusion | flops 1107558400 | bytes 42754048 | tf_op jit(solution)/shard_map/htu,hud->thd/dot_general | solution.py:97
  219.8 1.0 copy.106
  220.9 1.4 collective-permute-start.12
  222.3 1.0 collective-permute-start.7
  223.2 1.2 collective-permute-done.12
  224.5 2.6 collective-permute-start.13
  227.1 3.7 %fusion.50 = bf16[1,128,2048]{1,2,0:T(8,128)(2,1)S(1)} fusion(f32[2048]{0:T(1024)S(1)} %bitcast.153, f32[2048]{0:T(1024)S(1)} %bitcast.155, f32[2048]{0:T(1024)S(1)} %bitcast.145, bf16[128,2048]{0,1:T(8,128)(2,1)S(1)} %bitcast.126, f32[2048]{0:T(1024)S(1)} %bitcast.147, f32[2048]{0:T(1024)S(1)} %bitcast.149, f32[2048]{0:T(1024)S(1)} %bitcast.151, ...), kind=kLoop, calls=%fused_computation.93 | loop fusion | flops 10223616 | bytes 1130496 | tf_op jit(solution)/shard_map/broadcast_in_dim | solution.py:131
  230.8 1.0 copy.105
  231.8 3.7 %collective-permute-start.14 = (f32[7,2048]{1,0:T(8,128)S(1)}, f32[7,2048]{1,0:T(8,128)S(1)}, u32[]{:S(2)}, u32[]{:S(2)}) collective-permute-start(f32[7,2048]{1,0:T(8,128)S(1)} %add.89), channel_id=1, source_target_pairs={{0,64},{1,65},{2,66},{3,67},{4,68},{5,69},{6,70},{7,71},{8,72},{9,... | collective-permute-start | bytes 172040 | tf_op jit(solution)/shard_map/ppermute | solution.py:26
  235.6 3.3 %collective-permute-done.14 = f32[7,2048]{1,0:T(8,128)S(1)} collective-permute-done((f32[7,2048]{1,0:T(8,128)S(1)}, f32[7,2048]{1,0:T(8,128)S(1)}, u32[]{:S(2)}, u32[]{:S(2)}) %collective-permute-start.14) | collective-permute-done | bytes 57376 | tf_op jit(solution)/shard_map/ppermute | solution.py:26
  238.9 2.7 collective-permute-start.15
  241.6 15.0 %fusion = f32[16,128,2048]{1,2,0:T(8,128)} fusion(f32[16,2048]{1,0:T(8,128)S(1)} %get-tuple-element.53, f32[16,2048]{1,0:T(8,128)S(1)} %get-tuple-element.54, pred[128,2048]{0,1:T(8,128)(4,1)} %get-tuple-element.62, bf16[16,2048,128]{2,1,0:T(8,128)(2,1)} %all-gather.9.cloned.1.call-done, bf16[128,16,128]{2,1,0:T(8,128)(2,1)S(1)} %bitcast.131), kind=kOutput, calls=%fused_computation.1 | convolution fusion | flops 1090519040 | bytes 26214400 | tf_op jit(solution)/shard_map/hud,htd->hut/dot_general | solution.py:108
  256.6 0.6 add.91
  257.2 7.9 %all-gather.11.cloned.1.call-done = bf16[16,2048,128]{2,1,0:T(8,128)(2,1)} async-done(((bf16[16,128,128]{2,1,0:T(8,128)(2,1)}), bf16[16,2048,128]{2,1,0:T(8,128)(2,1)}) %all-gather.11.cloned.1.call-update) | async-done | bytes 8388624 | tf_op jit(solution)/shard_map/all_gather | solution.py:91
  265.2 13.5 %fusion.19 = bf16[16,128,128]{2,1,0:T(8,128)(2,1)S(1)} fusion(bf16[16,2048,128]{2,1,0:T(8,128)(2,1)} %all-gather.9.cloned.1.call-done, f32[16,128,2048]{1,2,0:T(8,128)} %fusion, f32[16,2048]{1,0:T(8,128)S(1)} %get-tuple-element.52, bf16[16,2048,128]{2,1,0:T(8,128)(2,1)} %all-gather.11.cloned.1.call-done, bf16[128,16,128]{2,0,1:T(8,128)(2,1)S(1)} %copy-done), kind=kOutput, calls=%fused_computation.35 | convolution fusion | flops 2164523008 | bytes 34734080 | tf_op jit(solution)/shard_map/hut,htd->uhd/dot_general | solution.py:116
  278.7 1.0 copy.107
  279.7 10.9 %fusion.16 = bf16[16,128,128]{2,1,0:T(8,128)(2,1)S(1)} fusion(bf16[16,2048,128]{2,1,0:T(8,128)(2,1)} %all-gather.11.cloned.1.call-done, f32[16,128,2048]{1,2,0:T(8,128)} %fusion), kind=kOutput, calls=%fused_computation.34 | convolution fusion | flops 1078198272 | bytes 25690112 | tf_op jit(solution)/shard_map/hut,htd->uhd/dot_general | solution.py:117
  290.6 1.0 copy.108
  (34 shorter events, 0.3 us)
Async XLA Ops:
  7.2 62.1 %all-gather.5.cloned.1.call-start = ((), (), s32[]{:S(2)}) async-start(), calls=%async_computation | async-start | bytes 8912896 | tf_op jit(solution)/shard_map/all_gather | solution.py:70
  9.3 129.2 %all-gather.7.cloned.1.call-start = ((), (), s32[]{:S(2)}) async-start(), calls=%async_computation.1 | async-start | bytes 8912896 | tf_op jit(solution)/shard_map/all_gather | solution.py:72
  70.3 171.3 %all-gather.9.cloned.1.call-start = ((), (), s32[]{:S(2)}) async-start(), calls=%async_computation.2 | async-start | bytes 8912896 | tf_op jit(solution)/shard_map/all_gather | solution.py:85
  73.9 12.9 %copy-start.1 = (bf16[1,128,2048]{2,1,0:T(8,128)(2,1)S(1)}, bf16[1,128,2048]{2,1,0:T(8,128)(2,1)}, u32[]{:S(2)}) copy-start(bf16[1,128,2048]{2,1,0:T(8,128)(2,1)} %param.8) | copy-start | bytes 1572868
  73.9 15.3 %copy-start.2 = (f32[7,2048]{1,0:T(8,128)S(1)}, f32[7,2048]{1,0:T(8,128)}, u32[]{:S(2)}) copy-start(f32[7,2048]{1,0:T(8,128)} %param.9) | copy-start | bytes 172036
  86.7 178.4 %all-gather.11.cloned.1.call-start = ((), (), s32[]{:S(2)}) async-start(), calls=%async_computation.3 | async-start | bytes 8912896 | tf_op jit(solution)/shard_map/all_gather | solution.py:91
  87.3 24.3 %collective-permute-start.1 = (bf16[3,2048]{0,1:T(8,128)(2,1)S(1)}, bf16[3,2048]{0,1:T(8,128)(2,1)S(1)}, u32[]{:S(2)}, u32[]{:S(2)}) collective-permute-start(bf16[3,2048]{0,1:T(8,128)(2,1)S(1)} %get-tuple-element.51), channel_id=1, source_target_pairs={{0,1},{1,2},{2,3},{3,4},{4,5},{5,6},{6,7},{7,8},{8,9},{9,10},{10,1... | collective-permute-start | bytes 36872 | tf_op jit(solution)/shard_map/ppermute | solution.py:15
  88.7 26.3 %collective-permute-start = (bf16[3,2048]{0,1:T(8,128)(2,1)S(1)}, bf16[3,2048]{0,1:T(8,128)(2,1)S(1)}, u32[]{:S(2)}, u32[]{:S(2)}) collective-permute-start(bf16[3,2048]{0,1:T(8,128)(2,1)S(1)} %get-tuple-element.50), channel_id=1, source_target_pairs={{1,0},{2,1},{3,2},{4,3},{5,4},{6,5},{7,6},{8,7},{9,8},{10,9},{11,1... | collective-permute-start | bytes 36872 | tf_op jit(solution)/shard_map/ppermute | solution.py:16
  164.5 2.1 collective-permute-start.2
  165.7 20.7 %collective-permute-start.3 = (bf16[3,2048]{0,1:T(8,128)(2,1)}, bf16[3,2048]{0,1:T(8,128)(2,1)S(1)}, u32[]{:S(2)}, u32[]{:S(2)}) collective-permute-start(bf16[3,2048]{0,1:T(8,128)(2,1)} %copy.90), channel_id=1, source_target_pairs={{1,0},{2,1},{3,2},{4,3},{5,4},{6,5},{7,6},{8,7},{9,8},{10,9},{11,1... | collective-permute-start | bytes 36872 | tf_op jit(solution)/shard_map/ppermute | solution.py:16
  189.9 1.3 collective-permute-start.8
  190.1 1.6 collective-permute-start.4
  191.3 5.5 %collective-permute-start.9 = (f32[7,2048]{1,0:T(8,128)S(1)}, f32[7,2048]{1,0:T(8,128)S(1)}, u32[]{:S(2)}, u32[]{:S(2)}) collective-permute-start(f32[7,2048]{1,0:T(8,128)S(1)} %add.84), channel_id=1, source_target_pairs={{0,2},{1,3},{2,0},{3,1},{4,6},{5,7},{6,4},{7,5},{8,10},{9,11},{10,... | collective-permute-start | bytes 172040 | tf_op jit(solution)/shard_map/ppermute | solution.py:26
  191.6 7.3 %collective-permute-start.5 = (f32[256,3,16]{0,2,1:T(8,128)S(1)}, f32[256,3,16]{0,2,1:T(8,128)S(1)}, u32[]{:S(2)}, u32[]{:S(2)}) collective-permute-start(f32[256,3,16]{0,2,1:T(8,128)S(1)} %maximum_select_fusion.3), channel_id=1, source_target_pairs={{0,2},{1,3},{2,0},{3,1},{4,6},{5,7},{6,4},{7,5},{8,10},{9,11},{10,... | collective-permute-start | bytes 147464 | tf_op jit(solution)/shard_map/ppermute | solution.py:37
  196.8 3.6 %collective-permute-start.10 = (f32[7,2048]{1,0:T(8,128)S(1)}, f32[7,2048]{1,0:T(8,128)S(1)}, u32[]{:S(2)}, u32[]{:S(2)}) collective-permute-start(f32[7,2048]{1,0:T(8,128)S(1)} %add.85), channel_id=1, source_target_pairs={{0,4},{1,5},{2,6},{3,7},{4,0},{5,1},{6,2},{7,3},{8,12},{9,13},{10,... | collective-permute-start | bytes 172040 | tf_op jit(solution)/shard_map/ppermute | solution.py:26
  198.9 23.3 %collective-permute-start.6 = (f32[512,3,16]{0,2,1:T(8,128)S(1)}, f32[512,3,16]{0,2,1:T(8,128)S(1)}, u32[]{:S(2)}, u32[]{:S(2)}) collective-permute-start(f32[512,3,16]{0,2,1:T(8,128)S(1)} %maximum_select_fusion.2), channel_id=1, source_target_pairs={{0,4},{1,5},{2,6},{3,7},{4,0},{5,1},{6,2},{7,3},{8,12},{9,13},{10,... | collective-permute-start | bytes 294920 | tf_op jit(solution)/shard_map/ppermute | solution.py:37
  200.4 20.4 %collective-permute-start.11 = (f32[7,2048]{1,0:T(8,128)S(1)}, f32[7,2048]{1,0:T(8,128)S(1)}, u32[]{:S(2)}, u32[]{:S(2)}) collective-permute-start(f32[7,2048]{1,0:T(8,128)S(1)} %add.86), channel_id=1, source_target_pairs={{0,8},{1,9},{2,10},{3,11},{4,12},{5,13},{6,14},{7,15},{8,0},{9,1},... | collective-permute-start | bytes 172040 | tf_op jit(solution)/shard_map/ppermute | solution.py:26
  220.9 3.6 %collective-permute-start.12 = (f32[7,2048]{1,0:T(8,128)S(1)}, f32[7,2048]{1,0:T(8,128)S(1)}, u32[]{:S(2)}, u32[]{:S(2)}) collective-permute-start(f32[7,2048]{1,0:T(8,128)S(1)} %add.87), channel_id=1, source_target_pairs={{0,16},{1,17},{2,18},{3,19},{4,20},{5,21},{6,22},{7,23},{8,24},{9,... | collective-permute-start | bytes 172040 | tf_op jit(solution)/shard_map/ppermute | solution.py:26
  222.3 13.3 %collective-permute-start.7 = (f32[1024,3,16]{0,2,1:T(8,128)S(1)}, f32[1024,3,16]{0,2,1:T(8,128)S(1)}, u32[]{:S(2)}, u32[]{:S(2)}) collective-permute-start(f32[1024,3,16]{0,2,1:T(8,128)S(1)} %maximum_select_fusion.1), channel_id=1, source_target_pairs={{0,8},{1,9},{2,10},{3,11},{4,12},{5,13},{6,14},{7,15},{8,0},{9,1},... | collective-permute-start | bytes 589832 | tf_op jit(solution)/shard_map/ppermute | solution.py:37
  224.5 7.3 %collective-permute-start.13 = (f32[7,2048]{1,0:T(8,128)S(1)}, f32[7,2048]{1,0:T(8,128)S(1)}, u32[]{:S(2)}, u32[]{:S(2)}) collective-permute-start(f32[7,2048]{1,0:T(8,128)S(1)} %add.88), channel_id=1, source_target_pairs={{0,32},{1,33},{2,34},{3,35},{4,36},{5,37},{6,38},{7,39},{8,40},{9,... | collective-permute-start | bytes 172040 | tf_op jit(solution)/shard_map/ppermute | solution.py:26
  231.8 7.1 %collective-permute-start.14 = (f32[7,2048]{1,0:T(8,128)S(1)}, f32[7,2048]{1,0:T(8,128)S(1)}, u32[]{:S(2)}, u32[]{:S(2)}) collective-permute-start(f32[7,2048]{1,0:T(8,128)S(1)} %add.89), channel_id=1, source_target_pairs={{0,64},{1,65},{2,66},{3,67},{4,68},{5,69},{6,70},{7,71},{8,72},{9,... | collective-permute-start | bytes 172040 | tf_op jit(solution)/shard_map/ppermute | solution.py:26
  238.9 17.6 %collective-permute-start.15 = (f32[7,2048]{1,0:T(8,128)S(1)}, f32[7,2048]{1,0:T(8,128)S(1)}, u32[]{:S(2)}, u32[]{:S(2)}) collective-permute-start(f32[7,2048]{1,0:T(8,128)S(1)} %add.90), channel_id=1, source_target_pairs={{0,128},{1,129},{2,130},{3,131},{4,132},{5,133},{6,134},{7,135},{8... | collective-permute-start | bytes 172040 | tf_op jit(solution)/shard_map/ppermute | solution.py:26
  241.6 23.6 %copy-start = (bf16[128,16,128]{2,0,1:T(8,128)(2,1)S(1)}, bf16[128,16,128]{2,0,1:T(8,128)(2,1)}, u32[]{:S(2)}) copy-start(bf16[128,16,128]{2,0,1:T(8,128)(2,1)} %copy.81) | copy-start | bytes 1572868
Sparse Core Ops, SparseCore 0:
  10.4 58.8 all-gather.4
  71.7 66.7 all-gather.6
  140.3 63.5 all-gather.8
  205.5 59.5 all-gather.10
where the time goes:
time: 304 us; the launch traced here: 298 us
  waiting for transfers between devices  135 us (44%)
  matrix products  93 us (31%)
  other arithmetic  22.1 us (7%)
  starting transfers between devices  18.8 us (6%)
  local copies, waits for them, and re-layouts  15.5 us (5%)
  between operations  14.3 us (5%)
    all_gather x1, waiting for transfers between devices, on_device(): k_heads = lax.all_gather(head_major(local_k), 'seq', axis=1, tiled=True)  58.6 us
    ppermute x2, waiting for transfers between devices, padded(): after = lax.ppermute(value[:width], 'seq', down)  22.9 us
    ppermute x2, waiting for transfers between devices, padded(): before = lax.ppermute(value[length - width:], 'seq', up)  22.3 us
    dot_general x1, matrix products, on_device(): jnp.einsum('htu,hud->thd', dscore, k_heads, preferred_element_type=jnp.fl...  17.1 us
    dot_general x1, matrix products, on_device(): jnp.einsum('thd,hud->htu', d_heads, v_heads, preferred_element_type=jnp.f...  16 us
    dot_general x1, matrix products, on_device(): jnp.einsum('hud,htd->hut', kq_heads, qa_heads, preferred_element_type=jnp...  15 us
    dot_general x1, matrix products, on_device(): jnp.einsum('hut,htd->uhd', dscore_t, qa_heads, preferred_element_type=jnp...  13.5 us
    ppermute x8, starting transfers between devices, butterfly_sum(): value = value + lax.ppermute(value, axes, pairs)  13.2 us
  transfers between devices with their start and end apart: 20, of which 12 were waited for; matrix products, arithmetic and copies ran while one was open for 34% of the time, Pallas kernels for 0%

commit v1 on v0

--- a/solution.py
+++ b/solution.py
@@ -88,7 +88,10 @@
     probs = raw / row_total
     probs_low = probs.astype(jnp.bfloat16)
     probs_low, grad_attn2 = lax.optimization_barrier((probs_low, grad_attn))
-    da_heads = lax.all_gather(head_major(grad_attn2), "seq", axis=1, tiled=True)
+    da_heads = jnp.concatenate(
+        lax.all_to_all(jnp.stack([head_major(grad_attn2)] * lax.axis_size("seq")), "seq", 0, 0),
+        axis=1,
+    )
     attended = jnp.einsum("htu,hud->thd", probs_low, v_heads, preferred_element_type=jnp.float32)
     attn_out = attended.astype(jnp.bfloat16).reshape(tok_rows, channels)
     dprob = jnp.einsum("thd,hud->htu", d_heads, v_heads, preferred_element_type=jnp.float32)

time: 304 us -> 437 us (1.44)
  the two profiles are of different devices: /device:TPU:1 before, /device:TPU:6 now
where the time goes in v1:
time: 437 us; the launch traced here: 431 us
  waiting for transfers between devices  207 us (47%)
  matrix products  92.7 us (21%)
  starting transfers between devices  58 us (13%)
  local copies, waits for them, and re-layouts  31.2 us (7%)
  other arithmetic  27.8 us (6%)
  between operations  14.2 us (3%)
    ppermute x8, waiting for transfers between devices, butterfly_sum(): value = value + lax.ppermute(value, axes, pairs)  110 us
    all_gather x1, waiting for transfers between devices, on_device(): k_heads = lax.all_gather(head_major(local_k), 'seq', axis=1, tiled=True)  57.2 us
    ppermute x8, starting transfers between devices, butterfly_sum(): value = value + lax.ppermute(value, axes, pairs)  40.4 us
    ppermute x2, waiting for transfers between devices, padded(): before = lax.ppermute(value[length - width:], 'seq', up)  17.7 us
    dot_general x1, matrix products, on_device(): jnp.einsum('htu,hud->thd', dscore, k_heads, preferred_element_type=jnp.fl...  17.1 us
    dot_general x1, matrix products, on_device(): jnp.einsum('thd,hud->htu', d_heads, v_heads, preferred_element_type=jnp.f...  16 us
    dot_general x1, matrix products, on_device(): jnp.einsum('hud,htd->hut', kq_heads, qa_heads, preferred_element_type=jnp...  14.8 us
    all_gather x1, waiting for transfers between devices, on_device(): v_heads = lax.all_gather(head_major(local_v), 'seq', axis=1, tiled=True)  14.2 us
  transfers between devices with their start and end apart: 20, of which 11 were waited for; matrix products, arithmetic and copies ran while one was open for 26% of the time, Pallas kernels for 0%

profile of v1, /device:TPU:6, one launch (start us, length us, event | category | flops | bytes accessed | tf_op | source)
XLA Modules:
  0.0 431.1 jit_solution(1909299309948894390)
XLA Ops:
  7.2 1.1 copy.121
  8.4 0.9 copy.129
  9.3 0.0 all-gather.6.cloned.1.call-start
  9.4 1.3 copy.81
  10.7 57.2 %all-gather.4.cloned.1.call-done = bf16[16,2048,128]{2,1,0:T(8,128)(2,1)} async-done(((bf16[16,128,128]{2,1,0:T(8,128)(2,1)}), bf16[16,2048,128]{2,1,0:T(8,128)(2,1)}) %all-gather.4.cloned.1.call-update) | async-done | bytes 8388624 | tf_op jit(solution)/shard_map/all_gather | solution.py:70
  67.9 1.0 copy.82
  68.9 0.0 all-gather.8.cloned.1.call-start
  69.0 1.3 copy.84
  70.3 1.1 copy.122
  71.5 1.0 iota_compare_fusion
  72.5 11.8 %fusion.1 = (f32[16,128]{1,0:T(8,128)S(1)}, f32[16,2048,128]{2,1,0:T(8,128)}) fusion(pred[128,2048]{0,1:T(8,128)(4,1)S(1)} %get-tuple-element.63, bf16[16,2048,128]{2,1,0:T(8,128)(2,1)} %all-gather.4.cloned.1.call-done, bf16[128,16,128]{2,1,0:T(8,128)(2,1)S(1)} %bitcast.144), kind=kOutput, calls=%fused_computation.4 | convolution fusion | flops 1086322688 | bytes 25960448 | tf_op jit(solution)/shard_map/thd,hud->htu/dot_general | solution.py:80
  84.3 1.0 copy.97
  85.3 0.3 copy.85
  85.6 1.0 slice_bitcast_fusion.1
  86.6 0.2 collective-permute-start.1
  86.9 2.7 collective-permute-start
  89.6 0.2 copy.106
  89.8 17.7 %collective-permute-done.1 = bf16[3,2048]{0,1:T(8,128)(2,1)S(1)} collective-permute-done((bf16[3,2048]{0,1:T(8,128)(2,1)}, bf16[3,2048]{0,1:T(8,128)(2,1)S(1)}, u32[]{:S(2)}, u32[]{:S(2)}) %collective-permute-start.1) | collective-permute-done | bytes 12320 | tf_op jit(solution)/shard_map/ppermute | solution.py:15
  107.6 5.9 %fusion.33 = bf16[128,2048]{0,1:T(8,128)(2,1)S(1)} fusion(bf16[128,2048]{0,1:T(8,128)(2,1)S(1)} %bitcast.128, bf16[3,2048]{0,1:T(8,128)(2,1)S(1)} %collective-permute-done.1, bf16[3,2048]{0,1:T(8,128)(2,1)} %collective-permute-done, f32[2048]{0:T(1024)S(1)} %bitcast.156, f32[2048]{0:T(1024)S(1)} %bitcast.158, f32[2048]{0:T(1024)S(1)} %bitcast.148, ...), kind=kLoop, calls=%fused_computation.66 | loop fusion | flops 10223616 | bytes 1130496 | tf_op jit(solution)/shard_map/convert_element_type | solution.py:65
  113.4 9.5 %fusion.5 = f32[16,128]{1,0:T(8,128)S(1)} fusion(f32[16,2048,128]{2,1,0:T(8,128)} %get-tuple-element.65, f32[16,128]{1,0:T(8,128)S(1)} %get-tuple-element.64, pred[128,2048]{0,1:T(8,128)(4,1)S(1)} %get-tuple-element.63), kind=kLoop, calls=%fused_computation.11 | loop fusion | flops 16775168 | bytes 17055744 | tf_op jit(solution)/shard_map/reduce_sum | solution.py:87
  122.9 14.2 %all-gather.6.cloned.1.call-done = bf16[16,2048,128]{2,1,0:T(8,128)(2,1)} async-done(((bf16[16,128,128]{2,1,0:T(8,128)(2,1)}), bf16[16,2048,128]{2,1,0:T(8,128)(2,1)}) %all-gather.6.cloned.1.call-update) | async-done | bytes 8388624 | tf_op jit(solution)/shard_map/all_gather | solution.py:72
  137.1 16.0 %multiply_reduce_fusion = (f32[16,128]{1,0:T(8,128)S(1)}, bf16[16,128,2048]{1,2,0:T(8,128)(2,1)}, f32[16,128,2048]{1,2,0:T(8,128)}) fusion(f32[16,128]{1,0:T(8,128)S(1)} %fusion.5, f32[16,128]{1,0:T(8,128)S(1)} %get-tuple-element.64, f32[16,2048,128]{2,1,0:T(8,128)} %get-tuple-element.65, pred[128,2048]{0,1:T(8,128)(4,1)S(1)} %get-tuple-element.63, ...), kind=kOutput, calls=%fused_computation.9 | convolution fusion | flops 1103099904 | bytes 51142656 | tf_op jit(solution)/shard_map/thd,hud->htu/dot_general | solution.py:97
  153.1 8.6 %multiply_reduce_fusion.1 = (f32[16,128]{1,0:T(8,128)S(1)}, bf16[128,16,128]{2,0,1:T(8,128)(2,1)S(1)}) fusion(f32[128,16,128]{2,0,1:T(8,128)S(1)} %copy.106, bf16[16,2048,128]{2,1,0:T(8,128)(2,1)} %all-gather.6.cloned.1.call-done, bf16[16,128,2048]{1,2,0:T(8,128)(2,1)} %get-tuple-element.14), kind=kOutput, calls=%fused_computation.73 | convolution fusion | flops 1074788352 | bytes 18358272 | tf_op jit(solution)/shard_map/htu,hud->thd/dot_general | solution.py:95
  161.8 0.4 collective-permute-start.2
  162.1 1.1 copy.91
  163.2 2.9 collective-permute-start.3
  166.0 0.3 copy.89
  166.3 0.3 copy.98
  166.6 5.3 %stack.21 = bf16[16,16,128,128]{3,2,1,0:T(8,128)(2,1)} broadcast(bf16[16,128,128]{2,1,0:T(8,128)(2,1)S(1)} %copy.98), dimensions={1,2,3} | broadcast | bytes 8912896 | tf_op jit(solution)/shard_map/stack | solution.py:92
  172.0 6.4 %all-to-all-start = ((bf16[16,16,128,128]{3,2,1,0:T(8,128)(2,1)}), bf16[16,16,128,128]{3,2,1,0:T(8,128)(2,1)}, u32[]{:S(2)}, u32[]{:S(2)}) async-start(bf16[16,16,128,128]{3,2,1,0:T(8,128)(2,1)} %stack.21), calls=%async_computation | async-start | bytes 16777216 | tf_op jit(solution)/shard_map/all_to_all | solution.py:92
  178.3 0.3 copy.90
  178.7 7.3 %collective-permute-done.3 = bf16[3,2048]{0,1:T(8,128)(2,1)} collective-permute-done((bf16[3,2048]{0,1:T(8,128)(2,1)}, bf16[3,2048]{0,1:T(8,128)(2,1)}, u32[]{:S(2)}, u32[]{:S(2)}) %collective-permute-start.3) | collective-permute-done | bytes 12320 | tf_op jit(solution)/shard_map/ppermute | solution.py:16
  186.0 4.8 %fusion.39 = (f32[2048]{0:T(1024)S(1)}, f32[2048]{0:T(1024)S(1)}, f32[2048]{0:T(1024)S(1)}, f32[2048]{0:T(1024)S(1)}, f32[2048]{0:T(1024)S(1)}, /*index=5*/f32[2048]{0:T(1024)S(1)}) fusion(bf16[3,2048]{0,1:T(8,128)(2,1)} %collective-permute-done.3, bf16[128,2048]{0,1:T(8,128)(2,1)S(1)} %bitcast.130, bf16[1,128,2048]{1,2,0:T(8,128)(2,1)S(1)} %copy.85, ...), kind=kLoop, calls=%fused_computation.72 | loop fusion | flops 9687040 | bytes 1122304 | tf_op jit(solution)/shard_map/reduce_sum | solution.py:130
  190.8 0.1 stack.55
  190.9 21.9 %collective-permute-start.8 = (f32[7,2048]{1,0:T(8,128)S(1)}, f32[7,2048]{1,0:T(8,128)S(1)}, u32[]{:S(2)}, u32[]{:S(2)}) collective-permute-start(f32[7,2048]{1,0:T(8,128)S(1)} %stack.55), channel_id=1, source_target_pairs={{0,1},{1,0},{2,3},{3,2},{4,5},{5,4},{6,7},{7,6},{8,9},{9,8},{10,11... | collective-permute-start | bytes 172040 | tf_op jit(solution)/shard_map/ppermute | solution.py:26
  212.8 0.1 collective-permute-start.4
  212.9 0.8 collective-permute-done.8
  213.7 0.1 collective-permute-start.9
  213.8 0.2 collective-permute-done.4
  214.0 1.9 collective-permute-start.5
  215.9 72.0 %collective-permute-done.9 = f32[7,2048]{1,0:T(8,128)S(1)} collective-permute-done((f32[7,2048]{1,0:T(8,128)S(1)}, f32[7,2048]{1,0:T(8,128)S(1)}, u32[]{:S(2)}, u32[]{:S(2)}) %collective-permute-start.9) | collective-permute-done | bytes 57376 | tf_op jit(solution)/shard_map/ppermute | solution.py:26
  287.9 0.1 collective-permute-start.10
  288.0 0.8 collective-permute-done.5
  288.8 1.3 collective-permute-start.6
  290.1 32.7 %collective-permute-done.10 = f32[7,2048]{1,0:T(8,128)S(1)} collective-permute-done((f32[7,2048]{1,0:T(8,128)S(1)}, f32[7,2048]{1,0:T(8,128)S(1)}, u32[]{:S(2)}, u32[]{:S(2)}) %collective-permute-start.10) | collective-permute-done | bytes 57376 | tf_op jit(solution)/shard_map/ppermute | solution.py:26
  322.8 3.0 collective-permute-start.11
  325.9 17.1 %fusion.20 = bf16[16,128,128]{2,1,0:T(8,128)(2,1)S(1)} fusion(bf16[16,2048,128]{2,1,0:T(8,128)(2,1)} %all-gather.4.cloned.1.call-done, f32[16,128,2048]{1,2,0:T(8,128)} %get-tuple-element.66, f32[16,128]{1,0:T(8,128)S(1)} %get-tuple-element.46, f32[16,2048,128]{2,1,0:T(8,128)} %get-tuple-element.65, f32[16,128]{1,0:T(8,128)S(1)} %fusion.5, ...), kind=kOutput, calls=%fused_computation.37 | convolution fusion | flops 1107558400 | bytes 42754048 | tf_op jit(solution)/shard_map/htu,hud->thd/dot_general | solution.py:100
  343.0 1.0 copy.108
  344.0 1.0 collective-permute-start.12
  345.0 1.7 collective-permute-start.7
  346.7 1.7 collective-permute-done.12
  348.4 2.1 collective-permute-start.13
  350.5 5.8 %fusion.50 = bf16[1,128,2048]{1,2,0:T(8,128)(2,1)S(1)} fusion(f32[2048]{0:T(1024)S(1)} %bitcast.157, f32[2048]{0:T(1024)S(1)} %bitcast.159, f32[2048]{0:T(1024)S(1)} %bitcast.149, bf16[128,2048]{0,1:T(8,128)(2,1)S(1)} %bitcast.131, f32[2048]{0:T(1024)S(1)} %bitcast.151, f32[2048]{0:T(1024)S(1)} %bitcast.153, f32[2048]{0:T(1024)S(1)} %bitcast.155, ...), kind=kLoop, calls=%fused_computation.93 | loop fusion | flops 10223616 | bytes 1130496 | tf_op jit(solution)/shard_map/broadcast_in_dim | solution.py:134
  356.3 1.0 copy.107
  357.3 6.0 %collective-permute-start.14 = (f32[7,2048]{1,0:T(8,128)S(1)}, f32[7,2048]{1,0:T(8,128)S(1)}, u32[]{:S(2)}, u32[]{:S(2)}) collective-permute-start(f32[7,2048]{1,0:T(8,128)S(1)} %add.89), channel_id=1, source_target_pairs={{0,64},{1,65},{2,66},{3,67},{4,68},{5,69},{6,70},{7,71},{8,72},{9,... | collective-permute-start | bytes 172040 | tf_op jit(solution)/shard_map/ppermute | solution.py:26
  363.4 2.4 collective-permute-done.14
  365.8 6.2 %collective-permute-start.15 = (f32[7,2048]{1,0:T(8,128)S(1)}, f32[7,2048]{1,0:T(8,128)S(1)}, u32[]{:S(2)}, u32[]{:S(2)}) collective-permute-start(f32[7,2048]{1,0:T(8,128)S(1)} %add.90), channel_id=1, source_target_pairs={{0,128},{1,129},{2,130},{3,131},{4,132},{5,133},{6,134},{7,135},{8... | collective-permute-start | bytes 172040 | tf_op jit(solution)/shard_map/ppermute | solution.py:26
  372.1 14.8 %fusion = f32[16,128,2048]{1,2,0:T(8,128)} fusion(f32[16,2048]{1,0:T(8,128)S(1)} %get-tuple-element.53, f32[16,2048]{1,0:T(8,128)S(1)} %get-tuple-element.54, pred[128,2048]{0,1:T(8,128)(4,1)S(1)} %copy-done.2, bf16[16,2048,128]{2,1,0:T(8,128)(2,1)} %all-gather.8.cloned.1.call-done, bf16[128,16,128]{2,1,0:T(8,128)(2,1)S(1)} %bitcast.136), kind=kOutput, calls=%fused_computation.1 | convolution fusion | flops 1090519040 | bytes 26214400 | tf_op jit(solution)/shard_map/hud,htd->hut/dot_general | solution.py:111
  386.9 0.6 add.91
  387.5 10.3 %copy.99 = bf16[16,16,128,128]{3,2,1,0:T(8,128)(2,1)} copy(bf16[16,16,128,128]{3,2,0,1:T(8,128)(2,1)} %bitcast.40) | data formatting | bytes 16777216 | tf_op jit(solution)/shard_map/reshape | solution.py:91
  397.9 11.0 %fusion.16 = bf16[16,128,128]{2,1,0:T(8,128)(2,1)S(1)} fusion(bf16[16,2048,128]{2,1,0:T(8,128)(2,1)} %bitcast.125, f32[16,128,2048]{1,2,0:T(8,128)} %fusion), kind=kOutput, calls=%fused_computation.34 | convolution fusion | flops 1078198272 | bytes 25690112 | tf_op jit(solution)/shard_map/hut,htd->uhd/dot_general | solution.py:120
  408.9 13.4 %fusion.19 = bf16[16,128,128]{2,1,0:T(8,128)(2,1)S(1)} fusion(bf16[16,2048,128]{2,1,0:T(8,128)(2,1)} %all-gather.8.cloned.1.call-done, f32[16,128,2048]{1,2,0:T(8,128)} %fusion, f32[16,2048]{1,0:T(8,128)S(1)} %get-tuple-element.52, bf16[16,2048,128]{2,1,0:T(8,128)(2,1)} %bitcast.126, bf16[128,16,128]{2,0,1:T(8,128)(2,1)S(1)} %copy-done), kind=kOutput, calls=%fused_computation.35 | convolution fusion | flops 2164523008 | bytes 34734080 | tf_op jit(solution)/shard_map/hut,htd->uhd/dot_general | solution.py:119
  422.3 1.0 copy.109
  423.3 1.0 copy.110
  (37 shorter events, 0.3 us)
Async XLA Ops:
  7.2 60.7 %all-gather.4.cloned.1.call-start = ((), (), s32[]{:S(2)}) async-start(), calls=%async_computation.1 | async-start | bytes 8912896 | tf_op jit(solution)/shard_map/all_gather | solution.py:70
  9.3 127.8 %all-gather.6.cloned.1.call-start = ((), (), s32[]{:S(2)}) async-start(), calls=%async_computation.2 | async-start | bytes 8912896 | tf_op jit(solution)/shard_map/all_gather | solution.py:72
  68.9 303.1 %all-gather.8.cloned.1.call-start = ((), (), s32[]{:S(2)}) async-start(), calls=%async_computation.3 | async-start | bytes 8912896 | tf_op jit(solution)/shard_map/all_gather | solution.py:85
  72.5 12.8 %copy-start.1 = (bf16[1,128,2048]{2,1,0:T(8,128)(2,1)S(1)}, bf16[1,128,2048]{2,1,0:T(8,128)(2,1)}, u32[]{:S(2)}) copy-start(bf16[1,128,2048]{2,1,0:T(8,128)(2,1)} %param.8) | copy-start | bytes 1572868
  72.5 17.0 %copy-start.3 = (f32[7,2048]{1,0:T(8,128)S(1)}, f32[7,2048]{1,0:T(8,128)}, u32[]{:S(2)}) copy-start(f32[7,2048]{1,0:T(8,128)} %param.9) | copy-start | bytes 172036
  86.6 20.9 %collective-permute-start.1 = (bf16[3,2048]{0,1:T(8,128)(2,1)}, bf16[3,2048]{0,1:T(8,128)(2,1)S(1)}, u32[]{:S(2)}, u32[]{:S(2)}) collective-permute-start(bf16[3,2048]{0,1:T(8,128)(2,1)} %get-tuple-element.51), channel_id=1, source_target_pairs={{0,1},{1,2},{2,3},{3,4},{4,5},{5,6},{6,7},{7,8},{8,9},{9,10},{10,1... | collective-permute-start | bytes 36872 | tf_op jit(solution)/shard_map/ppermute | solution.py:15
  86.9 20.7 %collective-permute-start = (bf16[3,2048]{0,1:T(8,128)(2,1)S(1)}, bf16[3,2048]{0,1:T(8,128)(2,1)}, u32[]{:S(2)}, u32[]{:S(2)}) collective-permute-start(bf16[3,2048]{0,1:T(8,128)(2,1)S(1)} %get-tuple-element.50), channel_id=1, source_target_pairs={{1,0},{2,1},{3,2},{4,3},{5,4},{6,5},{7,6},{8,7},{9,8},{10,9},{11,1... | collective-permute-start | bytes 36872 | tf_op jit(solution)/shard_map/ppermute | solution.py:16
  161.8 16.6 %collective-permute-start.2 = (bf16[3,2048]{1,0:T(4,128)(2,1)S(1)}, bf16[3,2048]{1,0:T(4,128)(2,1)S(1)}, u32[]{:S(2)}, u32[]{:S(2)}) collective-permute-start(bf16[3,2048]{1,0:T(4,128)(2,1)S(1)} %get-tuple-element.49), channel_id=1, source_target_pairs={{0,1},{1,2},{2,3},{3,4},{4,5},{5,6},{6,7},{7,8},{8,9},{9,10},{10,1... | collective-permute-start | bytes 36872 | tf_op jit(solution)/shard_map/ppermute | solution.py:15
  163.2 22.8 %collective-permute-start.3 = (bf16[3,2048]{0,1:T(8,128)(2,1)}, bf16[3,2048]{0,1:T(8,128)(2,1)}, u32[]{:S(2)}, u32[]{:S(2)}) collective-permute-start(bf16[3,2048]{0,1:T(8,128)(2,1)} %copy.91), channel_id=1, source_target_pairs={{1,0},{2,1},{3,2},{4,3},{5,4},{6,5},{7,6},{8,7},{9,8},{10,9},{11,1... | collective-permute-start | bytes 36872 | tf_op jit(solution)/shard_map/ppermute | solution.py:16
  172.0 215.6 %all-to-all-start = ((bf16[16,16,128,128]{3,2,1,0:T(8,128)(2,1)}), bf16[16,16,128,128]{3,2,1,0:T(8,128)(2,1)}, u32[]{:S(2)}, u32[]{:S(2)}) async-start(bf16[16,16,128,128]{3,2,1,0:T(8,128)(2,1)} %stack.21), calls=%async_computation | async-start | bytes 16777216 | tf_op jit(solution)/shard_map/all_to_all | solution.py:92
  190.9 22.8 %collective-permute-start.8 = (f32[7,2048]{1,0:T(8,128)S(1)}, f32[7,2048]{1,0:T(8,128)S(1)}, u32[]{:S(2)}, u32[]{:S(2)}) collective-permute-start(f32[7,2048]{1,0:T(8,128)S(1)} %stack.55), channel_id=1, source_target_pairs={{0,1},{1,0},{2,3},{3,2},{4,5},{5,4},{6,7},{7,6},{8,9},{9,8},{10,11... | collective-permute-start | bytes 172040 | tf_op jit(solution)/shard_map/ppermute | solution.py:26
  212.8 1.2 collective-permute-start.4
  213.7 74.2 %collective-permute-start.9 = (f32[7,2048]{1,0:T(8,128)S(1)}, f32[7,2048]{1,0:T(8,128)S(1)}, u32[]{:S(2)}, u32[]{:S(2)}) collective-permute-start(f32[7,2048]{1,0:T(8,128)S(1)} %add.84), channel_id=1, source_target_pairs={{0,2},{1,3},{2,0},{3,1},{4,6},{5,7},{6,4},{7,5},{8,10},{9,11},{10,... | collective-permute-start | bytes 172040 | tf_op jit(solution)/shard_map/ppermute | solution.py:26
  214.0 74.8 %collective-permute-start.5 = (f32[256,3,16]{0,2,1:T(8,128)S(1)}, f32[256,3,16]{0,2,1:T(8,128)S(1)}, u32[]{:S(2)}, u32[]{:S(2)}) collective-permute-start(f32[256,3,16]{0,2,1:T(8,128)S(1)} %maximum_select_fusion.3), channel_id=1, source_target_pairs={{0,2},{1,3},{2,0},{3,1},{4,6},{5,7},{6,4},{7,5},{8,10},{9,11},{10,... | collective-permute-start | bytes 147464 | tf_op jit(solution)/shard_map/ppermute | solution.py:37
  287.9 34.9 %collective-permute-start.10 = (f32[7,2048]{1,0:T(8,128)S(1)}, f32[7,2048]{1,0:T(8,128)S(1)}, u32[]{:S(2)}, u32[]{:S(2)}) collective-permute-start(f32[7,2048]{1,0:T(8,128)S(1)} %add.85), channel_id=1, source_target_pairs={{0,4},{1,5},{2,6},{3,7},{4,0},{5,1},{6,2},{7,3},{8,12},{9,13},{10,... | collective-permute-start | bytes 172040 | tf_op jit(solution)/shard_map/ppermute | solution.py:26
  288.8 56.2 %collective-permute-start.6 = (f32[512,3,16]{0,2,1:T(8,128)S(1)}, f32[512,3,16]{0,2,1:T(8,128)S(1)}, u32[]{:S(2)}, u32[]{:S(2)}) collective-permute-start(f32[512,3,16]{0,2,1:T(8,128)S(1)} %maximum_select_fusion.2), channel_id=1, source_target_pairs={{0,4},{1,5},{2,6},{3,7},{4,0},{5,1},{6,2},{7,3},{8,12},{9,13},{10,... | collective-permute-start | bytes 294920 | tf_op jit(solution)/shard_map/ppermute | solution.py:37
  322.8 21.1 %collective-permute-start.11 = (f32[7,2048]{1,0:T(8,128)S(1)}, f32[7,2048]{1,0:T(8,128)S(1)}, u32[]{:S(2)}, u32[]{:S(2)}) collective-permute-start(f32[7,2048]{1,0:T(8,128)S(1)} %add.86), channel_id=1, source_target_pairs={{0,8},{1,9},{2,10},{3,11},{4,12},{5,13},{6,14},{7,15},{8,0},{9,1},... | collective-permute-start | bytes 172040 | tf_op jit(solution)/shard_map/ppermute | solution.py:26
  325.9 46.2 %copy-start.2 = (pred[128,2048]{0,1:T(8,128)(4,1)S(1)}, pred[128,2048]{0,1:T(8,128)(4,1)}, u32[]{:S(2)}) copy-start(pred[128,2048]{0,1:T(8,128)(4,1)} %get-tuple-element.62) | copy-start | bytes 786436
  344.0 4.4 %collective-permute-start.12 = (f32[7,2048]{1,0:T(8,128)S(1)}, f32[7,2048]{1,0:T(8,128)S(1)}, u32[]{:S(2)}, u32[]{:S(2)}) collective-permute-start(f32[7,2048]{1,0:T(8,128)S(1)} %add.87), channel_id=1, source_target_pairs={{0,16},{1,17},{2,18},{3,19},{4,20},{5,21},{6,22},{7,23},{8,24},{9,... | collective-permute-start | bytes 172040 | tf_op jit(solution)/shard_map/ppermute | solution.py:26
  345.0 18.3 %collective-permute-start.7 = (f32[1024,3,16]{0,2,1:T(8,128)S(1)}, f32[1024,3,16]{0,2,1:T(8,128)S(1)}, u32[]{:S(2)}, u32[]{:S(2)}) collective-permute-start(f32[1024,3,16]{0,2,1:T(8,128)S(1)} %maximum_select_fusion.1), channel_id=1, source_target_pairs={{0,8},{1,9},{2,10},{3,11},{4,12},{5,13},{6,14},{7,15},{8,0},{9,1},... | collective-permute-start | bytes 589832 | tf_op jit(solution)/shard_map/ppermute | solution.py:37
  348.4 9.0 %collective-permute-start.13 = (f32[7,2048]{1,0:T(8,128)S(1)}, f32[7,2048]{1,0:T(8,128)S(1)}, u32[]{:S(2)}, u32[]{:S(2)}) collective-permute-start(f32[7,2048]{1,0:T(8,128)S(1)} %add.88), channel_id=1, source_target_pairs={{0,32},{1,33},{2,34},{3,35},{4,36},{5,37},{6,38},{7,39},{8,40},{9,... | collective-permute-start | bytes 172040 | tf_op jit(solution)/shard_map/ppermute | solution.py:26
  357.3 8.5 %collective-permute-start.14 = (f32[7,2048]{1,0:T(8,128)S(1)}, f32[7,2048]{1,0:T(8,128)S(1)}, u32[]{:S(2)}, u32[]{:S(2)}) collective-permute-start(f32[7,2048]{1,0:T(8,128)S(1)} %add.89), channel_id=1, source_target_pairs={{0,64},{1,65},{2,66},{3,67},{4,68},{5,69},{6,70},{7,71},{8,72},{9,... | collective-permute-start | bytes 172040 | tf_op jit(solution)/shard_map/ppermute | solution.py:26
  365.8 21.1 %collective-permute-start.15 = (f32[7,2048]{1,0:T(8,128)S(1)}, f32[7,2048]{1,0:T(8,128)S(1)}, u32[]{:S(2)}, u32[]{:S(2)}) collective-permute-start(f32[7,2048]{1,0:T(8,128)S(1)} %add.90), channel_id=1, source_target_pairs={{0,128},{1,129},{2,130},{3,131},{4,132},{5,133},{6,134},{7,135},{8... | collective-permute-start | bytes 172040 | tf_op jit(solution)/shard_map/ppermute | solution.py:26
  397.9 11.0 %copy-start = (bf16[128,16,128]{2,0,1:T(8,128)(2,1)S(1)}, bf16[128,16,128]{2,0,1:T(8,128)(2,1)}, u32[]{:S(2)}) copy-start(bf16[128,16,128]{2,0,1:T(8,128)(2,1)} %copy.82) | copy-start | bytes 1572868
Sparse Core Ops, SparseCore 0:
  10.4 57.4 all-gather.3
  70.3 66.7 all-gather.5
  138.9 146.4 all-gather.7
